TPU v7x, 32 devices: a whole 2x2x4 slice. The times are simulated.
32 devices in a mesh: dp: 8 (over z, y), mp: 4 (over x, core).
Axes of the slice: x: 2, y: 2, z: 4, core: 2. Of those that a mesh axis runs over, the one named last changes fastest.
Arguments:
- gradients: bfloat16 [8, 4, 192, 16384], P('dp', 'mp'), may hold values from -3000 to 3000
- owner_list: int32 [192], replicated, may hold values from 0 to 7, as said below
- master_weights: float32 [4, 288, 16384], P('mp', 'dp'), may hold values from -6 to 6
- first_moment: float32 [4, 288, 16384], P('mp', 'dp'), may hold values from -6 to 6
- second_moment: float32 [4, 288, 16384], P('mp', 'dp'), may hold values from 0.05 to 2
- average_weights: float32 [4, 288, 16384], P('mp', 'dp'), may hold values from -6 to 6
Outputs:
- new_params: bfloat16 [4, 192, 16384], P('mp')
- new_master: float32 [4, 288, 16384], P('mp', 'dp')
- new_first: float32 [4, 288, 16384], P('mp', 'dp')
- new_second: float32 [4, 288, 16384], P('mp', 'dp')
- average_rows: float32 [4, 192, 16384], P('mp', 'dp')
Inputs may be any that keep to these rules, and one draw needn't show every extreme that they name: `owner_list`: each data rank owns at most 36 segments, and some rank owns exactly 36.
All inputs are finite; a program needn't handle non-finite values.
Results may differ from a plain program's by a relative error of at most 0.015.
Values may be sent and summed in bfloat16 or wider, within the bound.
No kernel may reach another device: no remote copies, remote signals or barrier semaphores. Data moves between devices by JAX's collectives and lax.ppermute only.
A program may use at most 128 MiB of HBM per device.

v0:
```python
import math
import jax
import jax.numpy as jnp
from jax import lax
from jax.sharding import PartitionSpec as P


def slot_matrix(owner_list, ranks, cap):
    count = owner_list.shape[0]
    position = jnp.arange(count, dtype=jnp.int32)
    same_owner = (owner_list[:, None] == owner_list[None, :]) & (
        position[None, :] < position[:, None]
    )
    slot_index = owner_list * cap + jnp.sum(same_owner.astype(jnp.int32), axis=1)
    rows = jnp.arange(ranks * cap, dtype=jnp.int32)
    return (rows[:, None] == slot_index[None, :]).astype(jnp.float32)


def on_device(gradients, owner_list, master_weights, first_moment, second_moment, average_weights):
    highest = lax.Precision.HIGHEST
    local_grad = gradients[0, 0]
    nseg, seg = local_grad.shape
    cap = master_weights.shape[1]
    ranks = lax.axis_size("dp")
    blocks = lax.axis_size("mp")
    per_rank = nseg // ranks
    my_rank = lax.axis_index("dp")
    placing = slot_matrix(owner_list, ranks, cap)
    my_slots = lax.dynamic_slice_in_dim(placing, my_rank * cap, cap, 0)
    in_use = jnp.sum(my_slots, axis=1)[:, None]
    summed = lax.psum(local_grad.astype(jnp.float32).astype(jnp.bfloat16), "dp").astype(jnp.float32)
    total_sq = lax.psum(jnp.sum(summed * summed), "mp")
    owned_grad = jnp.dot(my_slots, summed, precision=highest)
    clip_factor = jnp.minimum(1.0, math.sqrt(blocks * nseg * seg) / (jnp.sqrt(total_sq) + 1e-06))
    owned_grad = clip_factor * owned_grad
    new_first = in_use * (0.9 * first_moment[0] + 0.1 * owned_grad)
    new_second = in_use * (0.95 * second_moment[0] + 0.05 * owned_grad * owned_grad)
    first_hat = new_first / (1.0 - 0.9**20)
    second_hat = new_second / (1.0 - 0.95**20)
    old_master = master_weights[0]
    new_master = in_use * (
        old_master - 0.02 * (first_hat / (jnp.sqrt(second_hat) + 1e-08) + 0.1 * old_master)
    )
    averaged = 0.9 * average_weights[0] + 0.1 * new_master
    placing_rows = placing.T
    placing_half = placing_rows.astype(jnp.bfloat16)
    gathered = jnp.dot(
        placing_half,
        lax.all_gather(new_master.astype(jnp.bfloat16), "dp", axis=0, tiled=True),
        preferred_element_type=jnp.float32,
    )
    new_params = gathered.astype(jnp.bfloat16)
    spread_out = jnp.dot(my_slots.T, averaged, precision=highest).reshape(ranks, per_rank, seg)
    arrived = lax.all_to_all(spread_out, "dp", split_axis=0, concat_axis=0, tiled=True)
    average_rows = jnp.sum(arrived, axis=0)
    return (
        new_params[None],
        new_master[None],
        new_first[None],
        new_second[None],
        average_rows[None],
    )


def solution(mesh):
    return jax.shard_map(
        on_device,
        mesh=mesh,
        in_specs=(
            P("dp", "mp", None, None),
            P(),
            P("mp", "dp", None),
            P("mp", "dp", None),
            P("mp", "dp", None),
            P("mp", "dp", None),
        ),
        out_specs=(
            P("mp", None, None),
            P("mp", "dp", None),
            P("mp", "dp", None),
            P("mp", "dp", None),
            P("mp", "dp", None),
        ),
        check_vma=False,
    )
```

profile of v0, /device:TPU:0, one launch (start us, length us, event | category | flops | bytes accessed | tf_op | source)
XLA Modules:
  0.0 680.6 jit_solution(15627968808862761865)
XLA Ops:
  7.2 0.0 all-reduce.2.cloned.1.call-start
  7.2 0.0 copy-start.3
  7.2 0.7 all-reduce.2.cloned.1.call-update
  7.9 0.0 copy-done.3
  7.9 0.2 convert_reduce_fusion
  8.2 217.6 %all-reduce.2.cloned.1.call-done = bf16[192,16384]{1,0:T(8,128)(2,1)} async-done(((bf16[192,16384]{1,0:T(8,128)(2,1)}), bf16[192,16384]{1,0:T(8,128)(2,1)}) %all-reduce.2.cloned.1.call-update) | async-done | bytes 6291472 | tf_op jit(solution)/shard_map/psum | solution.py:31
  225.8 6.6 multiply_reduce_fusion
  232.4 0.1 convert_reduce_fusion.1
  232.5 7.7 %psum.15 = f32[]{:T(128)} all-reduce(f32[]{:T(128)} %multiply_reduce_fusion), channel_id=1, replica_groups=mesh['dp'=8,'mp'=4] {'mp'}, use_global_device_ids=true, to_apply=%region_4.0 | all-reduce | flops 1 | bytes 8 | tf_op jit(solution)/shard_map/psum | solution.py:32
  240.9 0.0 copy-start
  240.9 14.0 %convert_bitcast_fusion = (bf16[1,36,16384]{2,1,0:T(8,128)(2,1)}, f32[36,16384]{1,0:T(8,128)S(1)}, f32[1,36,16384]{2,1,0:T(8,128)}, f32[1,36,16384]{2,1,0:T(8,128)}) fusion(f32[1,36,16384]{2,0,1:T(1,128)} %param.10, f32[1,36,16384]{2,0,1:T(1,128)} %param.9, f32[1,36,16384]{2,0,1:T(1,128)} %param.8, f32[36]{0:T(128)S(1)} %convert_reduce_fusion.1, ...), kind=kOutput, calls=%fused_computation.20 | convolution fusion | flops 238288896 | bytes 21637640 | tf_op jit(solution)/shard_map/dot_general | solution.py:33
  254.9 0.0 copy-done
  254.9 8.4 %fusion.6 = f32[192,16384]{1,0:T(8,128)} fusion(f32[1,36,16384]{2,0,1:T(1,128)S(1)} %copy-done, f32[36,16384]{1,0:T(8,128)S(1)} %get-tuple-element.26, pred[288,192]{1,0:T(8,128)(4,1)S(1)} %iota_compare_fusion, s32[]{:T(128)S(6)} %select_n.3), kind=kOutput, calls=%fused_computation.13 | convolution fusion | flops 1360723968 | bytes 17573892 | tf_op jit(solution)/shard_map/dot_general | solution.py:53
  263.4 5.3 all-to-all-start
  268.7 0.3 all-gather.3.cloned.1.call-start
  269.0 0.5 all-gather.3.cloned.1.call-update
  269.5 0.0 copy-start.2
  269.5 3.8 copy.32
  273.3 0.0 copy-start.1
  273.3 0.0 copy-done.2
  273.3 3.8 copy.33
  277.2 0.0 copy-done.1
  277.2 3.8 copy.34
  281.0 362.5 %all-gather.3.cloned.1.call-done = bf16[8,36,16384]{2,1,0:T(8,128)(2,1)} async-done(((bf16[1,36,16384]{2,1,0:T(8,128)(2,1)}), bf16[8,36,16384]{2,1,0:T(8,128)(2,1)}) %all-gather.3.cloned.1.call-update) | async-done | bytes 9437200 | tf_op jit(solution)/shard_map/all_gather | solution.py:49
  643.5 8.5 %reshape.25 = bf16[288,16384]{1,0:T(8,128)(2,1)} reshape(bf16[8,36,16384]{2,1,0:T(8,128)(2,1)} %all-gather.3.cloned.1.call-done) | data formatting | bytes 18874368
  652.0 9.9 %fusion = bf16[1,192,16384]{2,1,0:T(8,128)(2,1)} fusion(bf16[288,16384]{1,0:T(8,128)(2,1)} %reshape.25, s32[192]{0:T(256)S(1)} %multiply_add_fusion), kind=kOutput, calls=%fused_computation.1 | convolution fusion | flops 1815250944 | bytes 15729408 | tf_op jit(solution)/shard_map/dot_general | solution.py:47
  661.8 5.4 all-to-all-done
  667.2 6.5 reduce_sum.39
  (2 shorter events, 0.1 us)
Async XLA Ops:
  7.2 218.6 %all-reduce.2.cloned.1.call-start = ((), (), s32[]{:S(2)}) async-start(), calls=%async_computation.1 | async-start | bytes 12582912 | tf_op jit(solution)/shard_map/psum | solution.py:31
  7.2 0.7 copy-start.3
  240.9 14.0 %copy-start = (f32[1,36,16384]{2,0,1:T(1,128)S(1)}, f32[1,36,16384]{2,0,1:T(1,128)}, u32[]{:S(2)}) copy-start(f32[1,36,16384]{2,0,1:T(1,128)} %param.11) | copy-start | bytes 7077892
  263.4 403.8 %all-to-all-start = ((f32[8,24,16384]{2,1,0:T(8,128)}), f32[8,24,16384]{2,1,0:T(8,128)}, u32[]{:S(2)}, u32[]{:S(2)}) async-start(f32[8,24,16384]{2,1,0:T(8,128)} %bitcast.45), calls=%async_computation | async-start | bytes 25165824 | tf_op jit(solution)/shard_map/all_to_all | solution.py:54
  268.7 374.8 %all-gather.3.cloned.1.call-start = ((), (), s32[]{:S(2)}) async-start(), calls=%async_computation.2 | async-start | bytes 11796480 | tf_op jit(solution)/shard_map/all_gather | solution.py:49
  269.5 3.8 copy-start.2
  273.3 3.8 copy-start.1
Sparse Core Ops, SparseCore 0:
  11.8 213.9 all-reduce.1
  272.6 370.8 all-gather.2
where the time goes:
time: 681 us
  waiting for transfers between devices  587 us (86%)
  matrix products  32.3 us (5%)
  local copies, waits for them, and re-layouts  20 us (3%)
  between operations  14.8 us (2%)
  other arithmetic  13.5 us (2%)
  blocking collectives  7.68 us (1%)
    all_gather x1, waiting for transfers between devices, on_device(): lax.all_gather(new_master.astype(jnp.bfloat16), 'dp', axis=0, tiled=True)  362 us
    psum x1, waiting for transfers between devices, on_device(): lax.psum(local_grad.astype(jnp.float32).astype(jnp.bfloat16), 'dp')  218 us
    unnamed x12, local copies, waits for them, and re-layouts  20 us
    dot_general x1, matrix products, on_device(): owned_grad = jnp.dot(my_slots, summed, precision=highest)  14 us
  transfers between devices with their start and end apart: 3, of which 3 were waited for; matrix products, arithmetic and copies ran while one was open for 4% of the time, Pallas kernels for 0%

commit v1 on v0

--- a/solution.py
+++ b/solution.py
@@ -1,8 +1,45 @@
+import functools
 import math
 import jax
 import jax.numpy as jnp
 from jax import lax
 from jax.sharding import PartitionSpec as P
+
+
+def test_kinds(local_block, axis_tag):
+    k_now = jax.lax.axis_index(axis_tag)
+    known = jax.lax.axis_size(axis_tag)
+    log = []
+    local_out, ready, s_next = (known, k_now, local_block.shape[0])
+    for hop_no, k in enumerate(local_block.shape):
+        log.append(k * local_out if hop_no == 0 else k)
+    block_out = jnp.zeros(log, local_block.dtype)
+    then = high = local_block
+    val = lax.dynamic_update_slice_in_dim(block_out, local_block, ready * s_next, axis=0)
+    it = 1
+    while it < local_out // 2 + 1:
+        pool = []
+        hop_no = 0
+        while hop_no < local_out:
+            pool.append((hop_no, (hop_no + 1) % local_out))
+            hop_no += 1
+        then = jax.lax.ppermute(then, axis_name=axis_tag, perm=pool)
+        val = lax.dynamic_update_slice_in_dim(val, then, (ready - it) % local_out * s_next, axis=0)
+        if 2 * it < local_out:
+            pile = []
+            hop_no = 0
+            while hop_no < local_out:
+                pile.append((hop_no, (hop_no - 1) % local_out))
+                hop_no += 1
+            high = jax.lax.ppermute(high, axis_name=axis_tag, perm=pile)
+            val = lax.dynamic_update_slice_in_dim(
+                val, high, (ready + it) % local_out * s_next, axis=0
+            )
+        it = it + 1
+    return val
+
+
+produce_ladders = functools.partial(test_kinds, axis_tag="dp")
 
 
 def slot_matrix(owner_list, ranks, cap):
@@ -46,7 +83,7 @@
     placing_half = placing_rows.astype(jnp.bfloat16)
     gathered = jnp.dot(
         placing_half,
-        lax.all_gather(new_master.astype(jnp.bfloat16), "dp", axis=0, tiled=True),
+        produce_ladders(new_master.astype(jnp.bfloat16)),
         preferred_element_type=jnp.float32,
     )
     new_params = gathered.astype(jnp.bfloat16)

time: 681 us -> 792 us (1.16)
  the two profiles are of different devices: /device:TPU:0 before, /device:TPU:10 now
where the time goes in v1:
time: 792 us; the launch traced here: 790 us
  waiting for transfers between devices  556 us (70%)
  local copies, waits for them, and re-layouts  84.1 us (11%)
  starting transfers between devices  82.3 us (10%)
  matrix products  32.4 us (4%)
  between operations  14.9 us (2%)
  other arithmetic  13.5 us (2%)
    ppermute x4, waiting for transfers between devices, test_kinds(): then = jax.lax.ppermute(then, axis_name=axis_tag, perm=pool)  341 us
    psum x1, waiting for transfers between devices, on_device(): lax.psum(local_grad.astype(jnp.float32).astype(jnp.bfloat16), 'dp')  214 us
    ppermute x4, starting transfers between devices, test_kinds(): then = jax.lax.ppermute(then, axis_name=axis_tag, perm=pool)  73 us
    dynamic_update_slice x4, local copies, waits for them, and re-layouts, test_kinds(): lax.dynamic_update_slice_in_dim(val, then, (ready - it) % local_out * s_n...  33.1 us
    dynamic_update_slice x3, local copies, waits for them, and re-layouts, test_kinds(): lax.dynamic_update_slice_in_dim(val, high, (ready + it) % local_out * s_n...  25.1 us
  transfers between devices with their start and end apart: 9, of which 4 were waited for; matrix products, arithmetic and copies ran while one was open for 12% of the time, Pallas kernels for 0%

profile of v1, /device:TPU:10, one launch (start us, length us, event | category | flops | bytes accessed | tf_op | source)
XLA Modules:
  0.0 790.2 jit_solution(17023939494790311582)
XLA Ops:
  7.2 0.0 all-reduce.2.cloned.1.call-start
  7.2 0.0 copy-start.8
  7.2 0.7 all-reduce.2.cloned.1.call-update
  7.9 0.0 copy-done.8
  7.9 0.2 convert_reduce_fusion
  8.2 214.5 %all-reduce.2.cloned.1.call-done = bf16[192,16384]{1,0:T(8,128)(2,1)} async-done(((bf16[192,16384]{1,0:T(8,128)(2,1)}), bf16[192,16384]{1,0:T(8,128)(2,1)}) %all-reduce.2.cloned.1.call-update) | async-done | bytes 6291472 | tf_op jit(solution)/shard_map/psum | solution.py:68
  222.6 6.6 multiply_reduce_fusion
  229.3 0.1 convert_reduce_fusion.1
  229.4 6.7 psum.15
  236.9 0.0 copy-start
  236.9 14.0 %fusion.21 = (bf16[36,16384]{1,0:T(8,128)(2,1)}, f32[36,16384]{1,0:T(8,128)S(1)}, f32[1,36,16384]{2,1,0:T(8,128)}, f32[1,36,16384]{2,1,0:T(8,128)}) fusion(f32[1,36,16384]{2,0,1:T(1,128)} %param.10, f32[1,36,16384]{2,0,1:T(1,128)} %param.9, f32[1,36,16384]{2,0,1:T(1,128)} %param.8, f32[36]{0:T(128)S(1)} %convert_reduce_fusion.1, ...), kind=kOutput, calls=%fused_computation.39 | convolution fusion | flops 238288896 | bytes 21637640 | tf_op jit(solution)/shard_map/dot_general | solution.py:70
  250.9 0.0 copy-done
  250.9 8.5 %fusion.6 = f32[192,16384]{1,0:T(8,128)} fusion(f32[1,36,16384]{2,0,1:T(1,128)S(1)} %copy-done, f32[36,16384]{1,0:T(8,128)S(1)} %get-tuple-element.16, pred[288,192]{1,0:T(8,128)(4,1)S(1)} %iota_compare_fusion, s32[]{:T(128)S(6)} %select_n.56), kind=kOutput, calls=%fused_computation.13 | convolution fusion | flops 1360723968 | bytes 17573892 | tf_op jit(solution)/shard_map/dot_general | solution.py:90
  259.4 7.4 all-to-all-start
  266.7 1.5 collective-permute-start
  268.2 1.5 collective-permute-start.1
  269.7 229.9 %collective-permute-done = bf16[36,16384]{1,0:T(8,128)(2,1)S(1)} collective-permute-done((bf16[36,16384]{1,0:T(8,128)(2,1)}, bf16[36,16384]{1,0:T(8,128)(2,1)S(1)}, u32[]{:S(2)}, u32[]{:S(2)}) %collective-permute-start) | collective-permute-done | bytes 1179680 | tf_op jit(solution)/shard_map/ppermute | solution.py:26
  499.5 0.0 copy-start.3
  499.5 1.1 copy-done.3
  500.6 66.5 %collective-permute-start.2 = (bf16[36,16384]{1,0:T(8,128)(2,1)S(1)}, bf16[36,16384]{1,0:T(8,128)(2,1)S(1)}, u32[]{:S(2)}, u32[]{:S(2)}) collective-permute-start(bf16[36,16384]{1,0:T(8,128)(2,1)S(1)} %collective-permute-done), channel_id=1, source_target_pairs={{0,4},{4,8},{8,12},{12,16},{16,20},{20,24},{24,28},{28,0},{1,5},{5... | collective-permute-start | bytes 3538952 | tf_op jit(solution)/shard_map/ppermute | solution.py:26
  567.1 0.0 collective-permute-done.1
  567.1 0.0 copy-start.4
  567.1 0.0 collective-permute-start.3
  567.1 56.3 %collective-permute-done.2 = bf16[36,16384]{1,0:T(8,128)(2,1)S(1)} collective-permute-done((bf16[36,16384]{1,0:T(8,128)(2,1)S(1)}, bf16[36,16384]{1,0:T(8,128)(2,1)S(1)}, u32[]{:S(2)}, u32[]{:S(2)}) %collective-permute-start.2) | collective-permute-done | bytes 1179680 | tf_op jit(solution)/shard_map/ppermute | solution.py:26
  623.4 0.0 copy-done.4
  623.4 0.0 copy-start.6
  623.4 2.5 collective-permute-start.4
  625.9 0.0 collective-permute-done.3
  625.9 0.0 copy-done.6
  625.9 0.4 collective-permute-start.5
  626.3 55.0 %collective-permute-done.4 = bf16[36,16384]{1,0:T(8,128)(2,1)} collective-permute-done((bf16[36,16384]{1,0:T(8,128)(2,1)S(1)}, bf16[36,16384]{1,0:T(8,128)(2,1)}, u32[]{:S(2)}, u32[]{:S(2)}) %collective-permute-start.4) | collective-permute-done | bytes 1179680 | tf_op jit(solution)/shard_map/ppermute | solution.py:26
  681.3 2.6 collective-permute-start.6
  683.9 4.7 broadcast_in_dim.12
  688.6 8.6 %dynamic_update_slice.24 = bf16[288,16384]{1,0:T(8,128)(2,1)} dynamic-update-slice(bf16[288,16384]{1,0:T(8,128)(2,1)} %broadcast_in_dim.12, bf16[36,16384]{1,0:T(8,128)(2,1)} %get-tuple-element.15, s32[]{:T(128)S(6)} %select_n.56, s32[]{:T(128)} %constant.66.clone.1) | dynamic-update-slice | bytes 2359300 | tf_op jit(solution)/shard_map/dynamic_update_slice | solution.py:18
  697.2 0.0 copy-start.2
  697.2 3.8 copy.20
  701.0 0.0 copy-start.1
  701.0 0.0 copy-done.2
  701.0 3.8 copy.21
  704.8 0.0 copy-done.1
  704.8 3.8 copy.22
  708.7 0.0 copy-start.5
  708.7 0.0 copy-start.7
  708.7 8.7 %dynamic_update_slice.25 = bf16[288,16384]{1,0:T(8,128)(2,1)} dynamic-update-slice(bf16[288,16384]{1,0:T(8,128)(2,1)} %dynamic_update_slice.24, bf16[36,16384]{1,0:T(8,128)(2,1)} %copy-done.3, s32[]{:T(128)S(6)} %select_n.58, s32[]{:T(128)} %constant.66.clone.1) | dynamic-update-slice | bytes 2359300 | tf_op jit(solution)/shard_map/dynamic_update_slice | solution.py:27
  717.4 0.0 copy-done.5
  717.4 8.0 %dynamic_update_slice.26 = bf16[288,16384]{1,0:T(8,128)(2,1)} dynamic-update-slice(bf16[288,16384]{1,0:T(8,128)(2,1)} %dynamic_update_slice.25, bf16[36,16384]{1,0:T(8,128)(2,1)S(1)} %copy-done.5, s32[]{:T(128)S(6)} %select_n.60, s32[]{:T(128)} %constant.66.clone.1) | dynamic-update-slice | bytes 2359300 | tf_op jit(solution)/shard_map/dynamic_update_slice | solution.py:35
  725.4 0.0 copy-done.7
  725.4 8.0 %dynamic_update_slice.27 = bf16[288,16384]{1,0:T(8,128)(2,1)} dynamic-update-slice(bf16[288,16384]{1,0:T(8,128)(2,1)} %dynamic_update_slice.26, bf16[36,16384]{1,0:T(8,128)(2,1)S(1)} %copy-done.7, s32[]{:T(128)S(6)} %select_n.62, s32[]{:T(128)} %constant.66.clone.1) | dynamic-update-slice | bytes 2359300 | tf_op jit(solution)/shard_map/dynamic_update_slice | solution.py:27
  733.3 8.6 %dynamic_update_slice.28 = bf16[288,16384]{1,0:T(8,128)(2,1)} dynamic-update-slice(bf16[288,16384]{1,0:T(8,128)(2,1)} %dynamic_update_slice.27, bf16[36,16384]{1,0:T(8,128)(2,1)} %collective-permute-done.3, s32[]{:T(128)S(6)} %select_n.64, s32[]{:T(128)} %constant.66.clone.1) | dynamic-update-slice | bytes 2359300 | tf_op jit(solution)/shard_map/dynamic_update_slice | solution.py:35
  741.9 7.9 dynamic_update_slice.29
  749.8 0.0 collective-permute-done.5
  749.8 8.6 %dynamic_update_slice.30 = bf16[288,16384]{1,0:T(8,128)(2,1)} dynamic-update-slice(bf16[288,16384]{1,0:T(8,128)(2,1)} %dynamic_update_slice.29, bf16[36,16384]{1,0:T(8,128)(2,1)} %collective-permute-done.5, s32[]{:T(128)S(6)} %select_n.68, s32[]{:T(128)} %constant.66.clone.1) | dynamic-update-slice | bytes 2359300 | tf_op jit(solution)/shard_map/dynamic_update_slice | solution.py:35
  758.4 0.0 collective-permute-done.6
  758.4 8.6 %dynamic_update_slice.31 = bf16[288,16384]{1,0:T(8,128)(2,1)} dynamic-update-slice(bf16[288,16384]{1,0:T(8,128)(2,1)} %dynamic_update_slice.30, bf16[36,16384]{1,0:T(8,128)(2,1)} %collective-permute-done.6, s32[]{:T(128)S(6)} %select_n.70, s32[]{:T(128)} %constant.66.clone.1) | dynamic-update-slice | bytes 2359300 | tf_op jit(solution)/shard_map/dynamic_update_slice | solution.py:27
  767.0 9.9 %fusion = bf16[1,192,16384]{2,1,0:T(8,128)(2,1)} fusion(bf16[288,16384]{1,0:T(8,128)(2,1)} %dynamic_update_slice.31, s32[192]{0:T(256)S(1)} %multiply_add_fusion), kind=kOutput, calls=%fused_computation.1 | convolution fusion | flops 1815250944 | bytes 15729408 | tf_op jit(solution)/shard_map/dot_general | solution.py:84
  776.8 0.0 all-to-all-done
  776.8 6.5 reduce_sum.39
  (2 shorter events, 0.1 us)
Async XLA Ops:
  7.2 215.5 %all-reduce.2.cloned.1.call-start = ((), (), s32[]{:S(2)}) async-start(), calls=%async_computation.1 | async-start | bytes 12582912 | tf_op jit(solution)/shard_map/psum | solution.py:68
  7.2 0.7 copy-start.8
  236.9 14.0 %copy-start = (f32[1,36,16384]{2,0,1:T(1,128)S(1)}, f32[1,36,16384]{2,0,1:T(1,128)}, u32[]{:S(2)}) copy-start(f32[1,36,16384]{2,0,1:T(1,128)} %param.11) | copy-start | bytes 7077892
  259.4 517.4 %all-to-all-start = ((f32[8,24,16384]{2,1,0:T(8,128)}), f32[8,24,16384]{2,1,0:T(8,128)}, u32[]{:S(2)}, u32[]{:S(2)}) async-start(f32[8,24,16384]{2,1,0:T(8,128)} %bitcast.43), calls=%async_computation | async-start | bytes 25165824 | tf_op jit(solution)/shard_map/all_to_all | solution.py:91
  266.7 232.8 %collective-permute-start = (bf16[36,16384]{1,0:T(8,128)(2,1)}, bf16[36,16384]{1,0:T(8,128)(2,1)S(1)}, u32[]{:S(2)}, u32[]{:S(2)}) collective-permute-start(bf16[36,16384]{1,0:T(8,128)(2,1)} %get-tuple-element.15), channel_id=1, source_target_pairs={{0,4},{4,8},{8,12},{12,16},{16,20},{20,24},{24,28},{28,0},{1,5},{5... | collective-permute-start | bytes 3538952 | tf_op jit(solution)/shard_map/ppermute | solution.py:26
  268.2 298.9 %collective-permute-start.1 = (bf16[36,16384]{1,0:T(8,128)(2,1)}, bf16[36,16384]{1,0:T(8,128)(2,1)S(1)}, u32[]{:S(2)}, u32[]{:S(2)}) collective-permute-start(bf16[36,16384]{1,0:T(8,128)(2,1)} %get-tuple-element.15), channel_id=1, source_target_pairs={{0,28},{4,0},{8,4},{12,8},{16,12},{20,16},{24,20},{28,24},{1,29},{... | collective-permute-start | bytes 3538952 | tf_op jit(solution)/shard_map/ppermute | solution.py:34
  499.5 1.1 copy-start.3
  500.6 122.8 %collective-permute-start.2 = (bf16[36,16384]{1,0:T(8,128)(2,1)S(1)}, bf16[36,16384]{1,0:T(8,128)(2,1)S(1)}, u32[]{:S(2)}, u32[]{:S(2)}) collective-permute-start(bf16[36,16384]{1,0:T(8,128)(2,1)S(1)} %collective-permute-done), channel_id=1, source_target_pairs={{0,4},{4,8},{8,12},{12,16},{16,20},{20,24},{24,28},{28,0},{1,5},{5... | collective-permute-start | bytes 3538952 | tf_op jit(solution)/shard_map/ppermute | solution.py:26
  567.1 56.3 %copy-start.4 = (bf16[36,16384]{1,0:T(8,128)(2,1)}, bf16[36,16384]{1,0:T(8,128)(2,1)S(1)}, u32[]{:S(2)}) copy-start(bf16[36,16384]{1,0:T(8,128)(2,1)S(1)} %collective-permute-done.1) | copy-start | bytes 3538948
  567.1 58.8 %collective-permute-start.3 = (bf16[36,16384]{1,0:T(8,128)(2,1)S(1)}, bf16[36,16384]{1,0:T(8,128)(2,1)}, u32[]{:S(2)}, u32[]{:S(2)}) collective-permute-start(bf16[36,16384]{1,0:T(8,128)(2,1)S(1)} %collective-permute-done.1), channel_id=1, source_target_pairs={{0,28},{4,0},{8,4},{12,8},{16,12},{20,16},{24,20},{28,24},{1,29},{... | collective-permute-start | bytes 3538952 | tf_op jit(solution)/shard_map/ppermute | solution.py:34
  623.4 2.5 copy-start.6
  623.4 57.9 %collective-permute-start.4 = (bf16[36,16384]{1,0:T(8,128)(2,1)S(1)}, bf16[36,16384]{1,0:T(8,128)(2,1)}, u32[]{:S(2)}, u32[]{:S(2)}) collective-permute-start(bf16[36,16384]{1,0:T(8,128)(2,1)S(1)} %collective-permute-done.2), channel_id=1, source_target_pairs={{0,4},{4,8},{8,12},{12,16},{16,20},{20,24},{24,28},{28,0},{1,5},{5... | collective-permute-start | bytes 3538952 | tf_op jit(solution)/shard_map/ppermute | solution.py:26
  625.9 123.9 %collective-permute-start.5 = (bf16[36,16384]{1,0:T(8,128)(2,1)}, bf16[36,16384]{1,0:T(8,128)(2,1)}, u32[]{:S(2)}, u32[]{:S(2)}) collective-permute-start(bf16[36,16384]{1,0:T(8,128)(2,1)} %collective-permute-done.3), channel_id=1, source_target_pairs={{0,28},{4,0},{8,4},{12,8},{16,12},{20,16},{24,20},{28,24},{1,29},{... | collective-permute-start | bytes 3538952 | tf_op jit(solution)/shard_map/ppermute | solution.py:34
  681.3 77.0 %collective-permute-start.6 = (bf16[36,16384]{1,0:T(8,128)(2,1)}, bf16[36,16384]{1,0:T(8,128)(2,1)}, u32[]{:S(2)}, u32[]{:S(2)}) collective-permute-start(bf16[36,16384]{1,0:T(8,128)(2,1)} %collective-permute-done.4), channel_id=1, source_target_pairs={{0,4},{4,8},{8,12},{12,16},{16,20},{20,24},{24,28},{28,0},{1,5},{5... | collective-permute-start | bytes 3538952 | tf_op jit(solution)/shard_map/ppermute | solution.py:26
  697.2 3.8 copy-start.2
  701.0 3.8 copy-start.1
  708.7 8.7 %copy-start.5 = (bf16[36,16384]{1,0:T(8,128)(2,1)S(1)}, bf16[36,16384]{1,0:T(8,128)(2,1)}, u32[]{:S(2)}) copy-start(bf16[36,16384]{1,0:T(8,128)(2,1)} %copy-done.4) | copy-start | bytes 3538948
  708.7 16.7 %copy-start.7 = (bf16[36,16384]{1,0:T(8,128)(2,1)S(1)}, bf16[36,16384]{1,0:T(8,128)(2,1)}, u32[]{:S(2)}) copy-start(bf16[36,16384]{1,0:T(8,128)(2,1)} %copy-done.6) | copy-start | bytes 3538948
Sparse Core Ops, SparseCore 0:
  11.8 210.8 all-reduce.1
